TPU v7x, 32 devices: a whole 2x2x4 slice. The times are simulated.
32 devices in a mesh: seq: 8 (over z, x), tp: 4 (over y, core).
Axes of the slice: x: 2, y: 2, z: 4, core: 2. Of those that a mesh axis runs over, the one named last changes fastest.
Arguments:
- hidden: bfloat16 [2048, 2048], P('seq', 'tp'), may hold values from -40 to 40
- new_queries: bfloat16 [2048, 2048], P('seq', 'tp'), may hold values from -9 to 9
- new_keys: bfloat16 [2048, 2048], P('seq', 'tp'), may hold values from -6 to 6
- new_values: bfloat16 [2048, 2048], P('seq', 'tp'), may hold values from -6 to 6
- cache_keys: bfloat16 [8, 4096, 2048], P('seq', None, 'tp'), may hold values from -6 to 6
- cache_values: bfloat16 [8, 4096, 2048], P('seq', None, 'tp'), may hold values from -6 to 6
- cache_lengths: int32 [8], replicated, may hold values from 1 to 4096, as said below
- out_proj: bfloat16 [2048, 2048], P('tp'), may hold values from -0.5 to 0.5
- moe_gain: float32 [2048], P('tp'), may hold values from 0.1 to 1.9
- expert_ids: int32 [2048, 8], P('seq'), may hold values from 0 to 15, all different within a row; in each aligned block of 256 rows (0 to 255, 256 to 511, ...) at most 192 rows name the same one
- route_weights: float32 [2048, 8], P('seq'), may hold values from 0.25 to 0.5
- expert_gate_up: bfloat16 [16, 2048, 2, 1024], P('seq', None, None, 'tp'), may hold values from -0.125 to 0.125
- expert_down: bfloat16 [16, 1024, 2048], P('seq', 'tp'), may hold values from -0.375 to 0.375
- next_gain: float32 [2048], P('tp'), may hold values from 0.1 to 1.9
- qkv_proj: bfloat16 [2048, 3, 2048], P(None, None, 'tp'), may hold values from -0.125 to 0.125
- query_gain: float32 [2048], P('tp'), may hold values from 0.1 to 1.9
- key_gain: float32 [2048], P('tp'), may hold values from 0.1 to 1.9
Outputs:
- layer_out: bfloat16 [2048, 2048], P('seq', 'tp')
- next_query: bfloat16 [2048, 2048], P('seq', 'tp')
- next_key: bfloat16 [2048, 2048], P('seq', 'tp')
- next_value: bfloat16 [2048, 2048], P('seq', 'tp')
Inputs may be any that keep to these rules, and one draw needn't show every extreme that they name: Request r has cached positions 0 to cache_lengths[r] - 1; one request has 4096 of them and one has 1. `expert_ids`: each row names 8 different experts; among the 256 rows of one request no expert is named more than 192 times, and in some request one expert is named exactly 192 times.
All inputs are finite; a program needn't handle non-finite values.
Results may differ from a plain program's by a relative error of at most 0.017.
Values may be sent and summed in bfloat16 or wider, within the bound.
No kernel may reach another device: no remote copies, remote signals or barrier semaphores. Data moves between devices by JAX's collectives and lax.ppermute only.
A program may use at most 128 MiB of HBM per device.

v0:
```python
import math
import jax
import jax.numpy as jnp
from jax import lax
from jax.sharding import PartitionSpec as P

D = 2048
HEAD_DIM = 128
TOP = 8
NEW = 256
epsilon = 1e-05


def softmax_parts(queries, key_rows, values, allowed):
    scores = jnp.einsum(
        "bthe,bche->bhtc", queries, key_rows, preferred_element_type=jnp.float32
    ) / math.sqrt(HEAD_DIM)
    scores = jnp.where(allowed[:, None], scores, -1e30)
    row_max = jnp.max(scores, axis=3)
    weights = jnp.where(allowed[:, None], jnp.exp(scores - row_max[..., None]), 0.0)
    row_total = jnp.sum(weights, axis=3)
    partial_out = jnp.einsum(
        "bhtc,bche->bthe", weights.astype(jnp.bfloat16), values, preferred_element_type=jnp.float32
    )
    return (partial_out, jnp.swapaxes(row_max, 1, 2), jnp.swapaxes(row_total, 1, 2))


def combine_parts(first, second):
    out_a, max_a, total_a = first
    out_b, max_b, total_b = second
    joint = jnp.maximum(max_a, max_b)
    factor_a = jnp.exp(max_a - joint)
    factor_b = jnp.exp(max_b - joint)
    return (
        out_a * factor_a[..., None] + out_b * factor_b[..., None],
        joint,
        total_a * factor_a + total_b * factor_b,
    )


def merge_parts(pieces, maxima, totals):
    overall = jnp.max(maxima, axis=0)
    factor = jnp.exp(maxima - overall[None])
    denominator = jnp.sum(totals * factor, axis=0)
    merged = jnp.sum(pieces * factor[..., None], axis=0)
    return merged / denominator[..., None]


def dense_experts(moe_in, expert_ids, route_weights, expert_gate_up, down_full, here, experts_all):
    local_experts = expert_gate_up.shape[0]
    hidden_quarter = expert_gate_up.shape[3]
    tokens, quarter = moe_in.shape
    seq_count = experts_all // local_experts
    gate_w = jnp.sum(
        route_weights[:, :, None]
        * (expert_ids[:, :, None] == jnp.arange(experts_all, dtype=jnp.int32)[None, None, :]),
        axis=1,
    )
    gate_t = jnp.transpose(gate_w)
    gate_hi = gate_t.astype(jnp.bfloat16)
    gate_lo = (gate_t - gate_hi.astype(jnp.float32)).astype(jnp.bfloat16)
    info = jnp.concatenate([gate_hi, gate_lo], axis=0).reshape(-1, quarter)
    packed = jnp.concatenate([moe_in, info], axis=0)
    gathered = lax.all_gather(packed, "seq", axis=0, tiled=False)
    rows_q = gathered[:, :tokens].reshape(seq_count * tokens, quarter)
    info_all = gathered[:, tokens:].reshape(seq_count, 2, experts_all, tokens).astype(jnp.float32)
    gate_all = info_all[:, 0] + info_all[:, 1]
    gate_local = lax.dynamic_slice_in_dim(gate_all, here * local_experts, local_experts, axis=1)
    gate_local = jnp.transpose(gate_local, (1, 0, 2)).reshape(local_experts, seq_count * tokens)
    rows = lax.all_gather(rows_q, "tp", axis=1, tiled=True)
    gate_up = expert_gate_up.reshape(local_experts, D, 2 * hidden_quarter)
    projected = jnp.einsum("td,edf->etf", rows, gate_up, preferred_element_type=jnp.float32)
    activated = jax.nn.silu(projected[..., :hidden_quarter]) * projected[..., hidden_quarter:]
    activated = activated.astype(jnp.bfloat16).astype(jnp.float32)
    weighted = (activated * gate_local[:, :, None]).astype(jnp.bfloat16)
    weighted = lax.all_gather(weighted, "tp", axis=2, tiled=True)
    partial = jnp.einsum(
        "etf,efd->td", weighted, down_full, preferred_element_type=jnp.float32
    ).astype(jnp.bfloat16)
    partial = lax.psum_scatter(partial, "seq", scatter_dimension=0, tiled=True)
    return partial.astype(jnp.float32)


def dispatch_experts(
    moe_in, expert_ids, route_weights, expert_gate_up, expert_down, experts_all, capacity
):
    quarter = moe_in.shape[1]
    local_experts = expert_gate_up.shape[0]
    flat_ids = expert_ids.reshape(NEW * TOP)
    onehot = (flat_ids[:, None] == jnp.arange(experts_all, dtype=jnp.int32)[None, :]).astype(
        jnp.int32
    )
    ranks = jnp.sum((jnp.cumsum(onehot, axis=0) - onehot) * onehot, axis=1)
    target = (flat_ids * capacity + ranks).reshape(NEW, TOP)
    slot_ids = jnp.arange(experts_all * capacity, dtype=jnp.int32)
    selector = jnp.sum(
        (target[None, :, :] == slot_ids[:, None, None]).astype(jnp.int32), axis=2
    ).astype(jnp.bfloat16)
    send_rows = jnp.dot(selector, moe_in, preferred_element_type=jnp.float32).astype(jnp.bfloat16)
    send_rows = send_rows.reshape(experts_all, capacity, quarter)
    received = lax.all_to_all(send_rows, "seq", split_axis=0, concat_axis=1, tiled=True)
    hidden_quarter = expert_gate_up.shape[3]
    gate_up_local = expert_gate_up.reshape(local_experts, D, 2 * hidden_quarter)
    weight_rows = gate_up_local
    projected = jnp.einsum(
        "erd,edf->erf",
        lax.all_gather(received, "tp", axis=2, tiled=True),
        weight_rows,
        preferred_element_type=jnp.float32,
    )
    activated = (
        jax.nn.silu(projected[..., :hidden_quarter]) * projected[..., hidden_quarter:]
    ).astype(jnp.bfloat16)
    down_terms = jnp.einsum(
        "erf,efd->erd", activated, expert_down, preferred_element_type=jnp.float32
    )
    expert_result = lax.psum_scatter(
        down_terms.astype(jnp.bfloat16), "tp", scatter_dimension=2, tiled=True
    )
    returned = lax.all_to_all(
        expert_result, "seq", split_axis=1, concat_axis=0, tiled=True
    ).reshape(experts_all * capacity, quarter)
    picked = jnp.take(returned, target, axis=0)
    return jnp.sum(route_weights[:, :, None] * picked.astype(jnp.float32), axis=1)


def body(
    hidden,
    new_queries,
    new_keys,
    new_values,
    cache_keys,
    cache_values,
    cache_lengths,
    out_proj,
    moe_gain,
    expert_ids,
    route_weights,
    expert_gate_up,
    expert_down,
    next_gain,
    qkv_proj,
    query_gain,
    key_gain,
):
    seq_count = lax.axis_size("seq")
    here = lax.axis_index("seq")
    local_experts = expert_gate_up.shape[0]
    experts_all = local_experts * seq_count
    capacity = max(2, 3 * NEW * TOP // (2 * experts_all))
    dense = NEW <= 2 * capacity
    if dense:
        tp_here = lax.axis_index("tp")
        quarter_width = hidden.shape[1]
        down_full = lax.all_gather(expert_down, "tp", axis=1, tiled=True)
        down_full = lax.dynamic_slice_in_dim(
            down_full, tp_here * quarter_width, quarter_width, axis=2
        )
    local_width = new_queries.shape[1]
    local_heads = local_width // HEAD_DIM
    quarter = hidden.shape[1]
    own_queries = new_queries.reshape(1, NEW, local_heads, HEAD_DIM)
    own_keys = new_keys.reshape(1, NEW, local_heads, HEAD_DIM)
    own_values = new_values.reshape(1, NEW, local_heads, HEAD_DIM)
    offsets = jnp.arange(NEW, dtype=jnp.int32)
    causal = (offsets[None, :] <= offsets[:, None])[None]
    own_out, own_max, own_total = softmax_parts(own_queries, own_keys, own_values, causal)
    span = cache_keys.shape[1]
    block = min(512, span)
    my_length = lax.dynamic_index_in_dim(cache_lengths, here, 0, keepdims=False)
    block_count = (my_length + block - 1) // block
    key_blocks = cache_keys.reshape(span, local_heads, HEAD_DIM)
    value_blocks = cache_values.reshape(span, local_heads, HEAD_DIM)

    def cache_block(index, carry):
        begin = index * block
        keys_here = lax.dynamic_slice_in_dim(key_blocks, begin, block, 0)[None]
        values_here = lax.dynamic_slice_in_dim(value_blocks, begin, block, 0)[None]
        positions = begin + jnp.arange(block, dtype=jnp.int32)
        allowed = jnp.broadcast_to((positions < my_length)[None, None, :], (1, NEW, block))
        return combine_parts(carry, softmax_parts(own_queries, keys_here, values_here, allowed))

    start_parts = (
        jnp.zeros((1, NEW, local_heads, HEAD_DIM), jnp.float32),
        jnp.full((1, NEW, local_heads), -1e30, jnp.float32),
        jnp.zeros((1, NEW, local_heads), jnp.float32),
    )
    pieces, maxima, totals = lax.fori_loop(0, block_count, cache_block, start_parts)
    attended = merge_parts(
        jnp.concatenate([own_out, pieces], 0),
        jnp.concatenate([own_max, maxima], 0),
        jnp.concatenate([own_total, totals], 0),
    )
    attended = attended.reshape(NEW, local_width).astype(jnp.bfloat16)
    if dense:
        attended, down_full = lax.optimization_barrier((attended, down_full))
    attn_term = jnp.dot(attended, out_proj, preferred_element_type=jnp.float32)
    residual = hidden.astype(jnp.float32) + lax.psum_scatter(
        attn_term.astype(jnp.bfloat16), "tp", scatter_dimension=1, tiled=True
    ).astype(jnp.float32)
    square_total = lax.psum(jnp.sum(residual * residual, axis=1), "tp")
    moe_in = (residual * lax.rsqrt(square_total / D + epsilon)[:, None] * moe_gain[None, :]).astype(
        jnp.bfloat16
    )
    if dense:
        moe_term = dense_experts(
            moe_in, expert_ids, route_weights, expert_gate_up, down_full, here, experts_all
        )
    else:
        moe_term = dispatch_experts(
            moe_in, expert_ids, route_weights, expert_gate_up, expert_down, experts_all, capacity
        )
    routed = residual + moe_term
    layer_out = routed.astype(jnp.bfloat16)
    scaled = (routed * next_gain[None, :]).astype(jnp.bfloat16)
    qkv_local = qkv_proj.reshape(D, 3 * local_width)
    weight_rows = qkv_local
    mixed = jnp.dot(
        lax.all_gather(scaled, "tp", axis=1, tiled=True),
        weight_rows,
        preferred_element_type=jnp.float32,
    )
    mixed = mixed.reshape(NEW, 3, local_width)
    squares_routed = jnp.sum(routed * routed, axis=1)
    routed_total, query_raw, key_raw = lax.psum(
        (
            squares_routed,
            jnp.sum(mixed[:, 0] * mixed[:, 0], axis=1),
            jnp.sum(mixed[:, 1] * mixed[:, 1], axis=1),
        ),
        "tp",
    )
    x_scale = lax.rsqrt(routed_total / D + epsilon)
    query_pre = mixed[:, 0] * x_scale[:, None]
    key_pre = mixed[:, 1] * x_scale[:, None]
    query_total = query_raw * x_scale * x_scale
    key_total = key_raw * x_scale * x_scale
    next_query = (
        query_pre * lax.rsqrt(query_total / D + epsilon)[:, None] * query_gain[None, :]
    ).astype(jnp.bfloat16)
    next_key = (key_pre * lax.rsqrt(key_total / D + epsilon)[:, None] * key_gain[None, :]).astype(
        jnp.bfloat16
    )
    next_value = (mixed[:, 2] * x_scale[:, None]).astype(jnp.bfloat16)
    return (layer_out, next_query, next_key, next_value)


def solution(mesh):
    return jax.shard_map(
        body,
        mesh=mesh,
        in_specs=(
            P("seq", "tp"),
            P("seq", "tp"),
            P("seq", "tp"),
            P("seq", "tp"),
            P("seq", None, "tp"),
            P("seq", None, "tp"),
            P(),
            P("tp", None),
            P("tp"),
            P("seq", None),
            P("seq", None),
            P("seq", None, None, "tp"),
            P("seq", "tp", None),
            P("tp"),
            P(None, None, "tp"),
            P("tp"),
            P("tp"),
        ),
        out_specs=(P("seq", "tp"), P("seq", "tp"), P("seq", "tp"), P("seq", "tp")),
        check_vma=False,
    )
```

profile of v0, /device:TPU:0, one launch (start us, length us, event | category | flops | bytes accessed | tf_op | source)
XLA Modules:
  0.0 412.0 jit_solution(3361592434585957795)
XLA Ops:
  9.6 6.4 %copy.95 = bf16[1,4096,512]{1,2,0:T(8,128)(2,1)} copy(bf16[1,4096,512]{2,1,0:T(8,128)(2,1)} %param.23) | data formatting | bytes 8388608 | tf_op args[4]
  16.0 6.6 %copy.97 = bf16[1,4096,512]{1,2,0:T(8,128)(2,1)} copy(bf16[1,4096,512]{2,1,0:T(8,128)(2,1)} %param.24) | data formatting | bytes 8388608 | tf_op args[5]
  22.7 28.9 %while.14 = (s32[]{:T(128)}, f32[1,256,4,128]{1,3,2,0:T(8,128)S(1)}, f32[1,256,4]{1,2,0:T(4,128)S(1)}, f32[1,256,4]{1,2,0:T(4,128)S(1)}, s32[]{:T(128)}, /*index...) while((s32[]{:T(128)}, ...), condition=%wide.region_4.5_spmd, body=%wide.region_1.4_spmd.sunk | while | flops 275651584 | bytes 8731323 | solution.py:188
  23.4 1.7 bitcast_reduce_fusion.2
  25.7 1.8 fusion.83
  28.2 1.6 bitcast_reduce_fusion.2
  30.5 1.8 fusion.83
  35.3 1.8 fusion.83
  40.1 1.8 fusion.83
  42.6 1.6 bitcast_reduce_fusion.2
  44.9 1.8 fusion.83
  49.7 1.8 fusion.83
  54.5 16.1 %all-gather.7.cloned.1.call-done = bf16[2,1024,2048]{2,1,0:T(8,128)(2,1)} async-done(((bf16[2,256,2048]{2,1,0:T(8,128)(2,1)}), bf16[2,1024,2048]{2,1,0:T(8,128)(2,1)}) %all-gather.7.cloned.1.call-update) | async-done | bytes 8388624 | tf_op jit(solution)/shard_map/all_gather | solution.py:155
  70.6 3.0 constant_dynamic-slice_fusion
  73.7 1.7 convolution_convert_fusion
  75.5 24.9 %reduce-scatter.3.cloned.1.call-done = bf16[256,512]{1,0:T(8,128)(2,1)} async-done(((bf16[256,2048]{1,0:T(8,128)(2,1)}), bf16[256,512]{1,0:T(8,128)(2,1)}) %reduce-scatter.3.cloned.1.call-update) | async-done | bytes 262160 | tf_op jit(solution)/shard_map/reduce_scatter | solution.py:198
  101.6 5.8 %psum.28 = f32[256]{0:T(256)S(1)} all-reduce(f32[256]{0:T(256)S(1)} %multiply_reduce_fusion.3), channel_id=1, replica_groups=mesh['seq'=8,'tp'=4] {'tp'}, use_global_device_ids=true, to_apply=%region_10.11 | all-reduce | flops 256 | bytes 2048 | tf_op jit(solution)/shard_map/psum | solution.py:201
  109.2 51.9 %all-gather.15.cloned.1.call-done = bf16[2176,512]{1,0:T(8,128)(2,1)} async-done(((bf16[272,512]{1,0:T(8,128)(2,1)}), bf16[2176,512]{1,0:T(8,128)(2,1)}) %all-gather.15.cloned.1.call-update) | async-done | bytes 2228240 | tf_op jit(solution)/shard_map/all_gather | solution.py:64
  161.1 3.1 slice.40
  164.2 7.8 %reshape.166 = bf16[2,2048,512]{2,1,0:T(8,128)(2,1)} reshape(bf16[2,2048,2,256]{3,2,1,0:T(2,128)(2,1)} %param.30) | data formatting | bytes 8388608 | tf_op jit(solution)/shard_map/reshape | solution.py:71
  173.1 48.0 %all-gather.9.cloned.1.call-done = bf16[2048,2048]{1,0:T(8,128)(2,1)} async-done(((bf16[2048,512]{1,0:T(8,128)(2,1)}), bf16[2048,2048]{1,0:T(8,128)(2,1)}) %all-gather.9.cloned.1.call-update) | async-done | bytes 8388624 | tf_op jit(solution)/shard_map/all_gather | solution.py:70
  221.1 12.4 %fusion.29 = f32[2,2048,512]{2,1,0:T(8,128)S(1)} fusion(bf16[2,2048,512]{2,1,0:T(8,128)(2,1)} %reshape.166, bf16[2048,2048]{1,0:T(8,128)(2,1)} %all-gather.9.cloned.1.call-done), kind=kOutput, calls=%fused_computation.37 | convolution fusion | flops 8589934592 | bytes 20971520 | tf_op jit(solution)/shard_map/td,edf->etf/dot_general | solution.py:72
  233.6 2.2 multiply_convert_fusion
  236.0 59.3 %all-gather.11.cloned.1.call-done = bf16[2,2048,1024]{2,1,0:T(8,128)(2,1)} async-done(((bf16[2,2048,256]{2,1,0:T(8,128)(2,1)}), bf16[2,2048,1024]{2,1,0:T(8,128)(2,1)}) %all-gather.11.cloned.1.call-update) | async-done | bytes 8388624 | tf_op jit(solution)/shard_map/all_gather | solution.py:76
  295.3 9.1 %bitcast_convert_fusion = bf16[2048,512]{1,0:T(8,128)(2,1)} fusion(bf16[2,2048,1024]{2,1,0:T(8,128)(2,1)} %all-gather.11.cloned.1.call-done, bf16[2,1024,512]{2,1,0:T(8,128)(2,1)S(1)} %copy-done.5), kind=kOutput, calls=%fused_computation.40 | convolution fusion | flops 4296015872 | bytes 12582912 | tf_op jit(solution)/shard_map/etf,efd->td/dot_general | solution.py:77
  304.5 68.0 %reduce-scatter.5.cloned.1.call-done = bf16[256,512]{1,0:T(8,128)(2,1)} async-done(((bf16[2048,512]{1,0:T(8,128)(2,1)}), bf16[256,512]{1,0:T(8,128)(2,1)}) %reduce-scatter.5.cloned.1.call-update) | async-done | bytes 262160 | tf_op jit(solution)/shard_map/reduce_scatter | solution.py:80
  372.5 1.9 multiply_reduce_fusion.2
  374.4 8.9 %copy.103 = bf16[2048,3,512]{0,2,1:T(8,128)(2,1)} copy(bf16[2048,3,512]{2,0,1:T(8,128)(2,1)} %param.33) | data formatting | bytes 12582912 | tf_op args[14]
  383.3 7.1 %all-gather.13.cloned.1.call-done = bf16[256,2048]{1,0:T(8,128)(2,1)} async-done(((bf16[256,512]{1,0:T(8,128)(2,1)}), bf16[256,2048]{1,0:T(8,128)(2,1)}) %all-gather.13.cloned.1.call-update) | async-done | bytes 1048592 | tf_op jit(solution)/shard_map/all_gather | solution.py:219
  390.4 5.1 %fusion.27 = f32[256,3,512]{2,0,1:T(8,128)S(1)} fusion(bf16[2048,3,512]{0,2,1:T(8,128)(2,1)} %copy.103, bf16[256,2048]{1,0:T(8,128)(2,1)} %all-gather.13.cloned.1.call-done), kind=kOutput, calls=%fused_computation.35 | convolution fusion | flops 1610612736 | bytes 8912896 | tf_op jit(solution)/shard_map/dot_general | solution.py:218
  396.8 5.9 %all-reduce = (f32[256]{0:T(256)S(1)}, f32[256]{0:T(256)S(1)}, f32[256]{0:T(256)S(1)}) all-reduce(f32[256]{0:T(256)S(1)} %get-tuple-element.107, f32[256]{0:T(256)S(1)} %get-tuple-element.142, f32[256]{0:T(256)S(1)} %get-tuple-element.106), channel_id=1, replica_groups=mesh['seq'=8,'tp'=4] {'tp'}, use_global_device_ids=true, to_apply=%region_16.17 | all-reduce | flops 768 | bytes 6144 | tf_op jit(solution)/shard_map/psum | solution.py:225
  402.7 2.4 fusion.40
  (109 shorter events, 23.0 us)
Async XLA Ops:
  7.2 66.5 %copy-start = (bf16[512,2048]{1,0:T(8,128)(2,1)S(1)}, bf16[512,2048]{1,0:T(8,128)(2,1)}, u32[]{:S(2)}) copy-start(bf16[512,2048]{1,0:T(8,128)(2,1)} %param.26) | copy-start | bytes 6291460
  7.2 0.8 copy-start.14
  7.2 2.1 copy-start.6
  7.2 63.4 %all-gather.7.cloned.1.call-start = ((), (), s32[]{:S(2)}) async-start(), calls=%async_computation.2 | async-start | bytes 10485760 | tf_op jit(solution)/shard_map/all_gather | solution.py:155
  7.9 92.5 %reduce-scatter.3.cloned.1.call-start = ((), (), s32[]{:S(2)}) async-start(), calls=%async_computation.3 | async-start | bytes 1310720 | tf_op jit(solution)/shard_map/reduce_scatter | solution.py:198
  51.8 1.6 copy-start.7
  73.6 1.8 copy-start.8
  73.6 1.8 copy-start.9
  73.6 26.8 %copy-start.3 = (bf16[256,512]{1,0:T(8,128)(2,1)S(1)}, bf16[256,512]{1,0:T(8,128)(2,1)}, u32[]{:S(2)}) copy-start(bf16[256,512]{1,0:T(8,128)(2,1)} %param.19) | copy-start | bytes 786436
  73.7 33.7 %copy-start.10 = (f32[512]{0:T(512)S(1)}, f32[512]{0:T(512)}, u32[]{:S(2)}) copy-start(f32[512]{0:T(512)} %param.27) | copy-start | bytes 6148
  75.4 85.7 %all-gather.15.cloned.1.call-start = ((), (), s32[]{:S(2)}) async-start(), calls=%async_computation.8 | async-start | bytes 2506752 | tf_op jit(solution)/shard_map/all_gather | solution.py:64
  109.1 111.9 %all-gather.9.cloned.1.call-start = ((), (), s32[]{:S(2)}) async-start(), calls=%async_computation.4 | async-start | bytes 10485760 | tf_op jit(solution)/shard_map/all_gather | solution.py:70
  164.1 131.2 %all-gather.11.cloned.1.call-start = ((), (), s32[]{:S(2)}) async-start(), calls=%async_computation.5 | async-start | bytes 10485760 | tf_op jit(solution)/shard_map/all_gather | solution.py:76
  235.7 59.6 %copy-start.5 = (bf16[2,1024,512]{2,1,0:T(8,128)(2,1)S(1)}, bf16[2,1024,512]{2,1,0:T(8,128)(2,1)}, u32[]{:S(2)}) copy-start(bf16[2,1024,512]{2,1,0:T(8,128)(2,1)} %constant_dynamic-slice_fusion) | copy-start | bytes 6291460
  235.8 136.7 %reduce-scatter.5.cloned.1.call-start = ((), (), s32[]{:S(2)}) async-start(), calls=%async_computation.6 | async-start | bytes 2359296 | tf_op jit(solution)/shard_map/reduce_scatter | solution.py:80
  304.4 68.0 %copy-start.4 = (bf16[256,512]{1,0:T(8,128)(2,1)S(1)}, bf16[256,512]{1,0:T(8,128)(2,1)}, u32[]{:S(2)}) copy-start(bf16[256,512]{1,0:T(8,128)(2,1)} %reduce-scatter.3.cloned.1.call-done) | copy-start | bytes 786436
  304.4 68.0 %copy-start.11 = (f32[512]{0:T(512)S(1)}, f32[512]{0:T(512)}, u32[]{:S(2)}) copy-start(f32[512]{0:T(512)} %param.32) | copy-start | bytes 6148
  304.5 86.0 %all-gather.13.cloned.1.call-start = ((), (), s32[]{:S(2)}) async-start(), calls=%async_computation.7 | async-start | bytes 1310720 | tf_op jit(solution)/shard_map/all_gather | solution.py:219
  383.3 19.4 %copy-start.12 = (f32[512]{0:T(512)S(1)}, f32[512]{0:T(512)}, u32[]{:S(2)}) copy-start(f32[512]{0:T(512)} %param.35) | copy-start | bytes 6148
  383.3 19.4 %copy-start.13 = (f32[512]{0:T(512)S(1)}, f32[512]{0:T(512)}, u32[]{:S(2)}) copy-start(f32[512]{0:T(512)} %param.34) | copy-start | bytes 6148
  390.4 14.7 %copy-start.1 = (bf16[512,2048]{1,0:T(8,128)(2,1)S(1)}, bf16[512,2048]{1,0:T(8,128)(2,1)}, u32[]{:S(2)}) copy-start(bf16[512,2048]{1,0:T(8,128)(2,1)} %param.26) | copy-start | bytes 6291460
  395.5 1.2 copy-start.2
Sparse Core Ops, SparseCore 0:
  9.6 60.9 all-gather.6
  75.5 24.8 reduce-scatter.2
  109.3 51.7 all-gather.14
  164.3 56.7 all-gather.8
  235.9 59.3 all-gather.10
  304.6 67.8 reduce-scatter.4
  374.7 15.6 all-gather.12
where the time goes:
time: 414 us; the launch traced here: 412 us
  waiting for transfers between devices  276 us (67%)
  matrix products  50.8 us (12%)
  local copies, waits for them, and re-layouts  38.4 us (9%)
  other arithmetic  19.2 us (5%)
  between operations  15.1 us (4%)
  blocking collectives  11.7 us (3%)
    reduce_scatter x1, waiting for transfers between devices, dense_experts(): partial = lax.psum_scatter(partial, 'seq', scatter_dimension=0, tiled=True)  68 us
    all_gather x1, waiting for transfers between devices, dense_experts(): weighted = lax.all_gather(weighted, 'tp', axis=2, tiled=True)  59.3 us
    all_gather x1, waiting for transfers between devices, dense_experts(): gathered = lax.all_gather(packed, 'seq', axis=0, tiled=False)  51.9 us
    all_gather x1, waiting for transfers between devices, dense_experts(): rows = lax.all_gather(rows_q, 'tp', axis=1, tiled=True)  48 us
    reduce_scatter x1, waiting for transfers between devices, body(): lax.psum_scatter(attn_term.astype(jnp.bfloat16), 'tp', scatter_dimension=...  24.9 us
    unnamed x35, local copies, waits for them, and re-layouts  23.3 us
    all_gather x1, waiting for transfers between devices, body(): down_full = lax.all_gather(expert_down, 'tp', axis=1, tiled=True)  16.1 us
    dot_general x1, matrix products, dense_experts(): jnp.einsum('td,edf->etf', rows, gate_up, preferred_element_type=jnp.float32)  12.4 us
  transfers between devices with their start and end apart: 7, of which 7 were waited for; matrix products, arithmetic and copies ran while one was open for 15% of the time, Pallas kernels for 0%

commit v1 on v0

--- a/solution.py
+++ b/solution.py
@@ -73,7 +73,12 @@
     activated = jax.nn.silu(projected[..., :hidden_quarter]) * projected[..., hidden_quarter:]
     activated = activated.astype(jnp.bfloat16).astype(jnp.float32)
     weighted = (activated * gate_local[:, :, None]).astype(jnp.bfloat16)
-    weighted = lax.all_gather(weighted, "tp", axis=2, tiled=True)
+    ring = [weighted]
+    for hop in range(3):
+        ring.append(lax.ppermute(ring[-1], "tp", [(dev, (dev + 1) % 4) for dev in range(4)]))
+    weighted = jnp.roll(
+        jnp.concatenate(ring[::-1], axis=2), (lax.axis_index("tp") + 1) * ring[0].shape[2], axis=2
+    )
     partial = jnp.einsum(
         "etf,efd->td", weighted, down_full, preferred_element_type=jnp.float32
     ).astype(jnp.bfloat16)

time: 414 us -> 440 us (1.063)
  local copies, waits for them, and re-layouts: 38.4 us -> 53 us
  waiting for transfers between devices: 276 us -> 288 us
    ppermute x0 -> x3, waiting for transfers between devices: none -> 76.5 us  [dense_experts(): lax.ppermute(ring[-1], 'tp', [(dev, (dev + 1) % 4) for dev in range(4)])]
    all_gather x1 -> x0, waiting for transfers between devices: 59.3 us -> none  [dense_experts(): weighted = lax.all_gather(weighted, 'tp', axis=2, tiled=True)]
    unnamed x35 -> x41, local copies, waits for them, and re-layouts: 23.3 us -> 33.5 us
  transfers between devices with their start and end apart: 7 -> 9, of which waited for: 7 -> 9; matrix products, arithmetic and copies ran while one was open for 15% -> 16% of each run, Pallas kernels for 0% -> 0%
where the time goes in v1:
time: 440 us; the launch traced here: 438 us
  waiting for transfers between devices  288 us (65%)
  local copies, waits for them, and re-layouts  53 us (12%)
  matrix products  48.4 us (11%)
  other arithmetic  21 us (5%)
  between operations  15.2 us (3%)
  blocking collectives  11.7 us (3%)
    ppermute x3, waiting for transfers between devices, dense_experts(): lax.ppermute(ring[-1], 'tp', [(dev, (dev + 1) % 4) for dev in range(4)])  76.5 us
    reduce_scatter x1, waiting for transfers between devices, dense_experts(): partial = lax.psum_scatter(partial, 'seq', scatter_dimension=0, tiled=True)  67.9 us
    all_gather x1, waiting for transfers between devices, dense_experts(): gathered = lax.all_gather(packed, 'seq', axis=0, tiled=False)  51.9 us
    all_gather x1, waiting for transfers between devices, dense_experts(): rows = lax.all_gather(rows_q, 'tp', axis=1, tiled=True)  44.3 us
    unnamed x41, local copies, waits for them, and re-layouts  33.5 us
    reduce_scatter x1, waiting for transfers between devices, body(): lax.psum_scatter(attn_term.astype(jnp.bfloat16), 'tp', scatter_dimension=...  24.9 us
    all_gather x1, waiting for transfers between devices, body(): down_full = lax.all_gather(expert_down, 'tp', axis=1, tiled=True)  14.5 us
    dot_general x1, matrix products, dense_experts(): jnp.einsum('td,edf->etf', rows, gate_up, preferred_element_type=jnp.float32)  12.5 us
  transfers between devices with their start and end apart: 9, of which 9 were waited for; matrix products, arithmetic and copies ran while one was open for 16% of the time, Pallas kernels for 0%

profile of v1, /device:TPU:0, one launch (start us, length us, event | category | flops | bytes accessed | tf_op | source)
XLA Modules:
  0.0 438.0 jit_solution(4071946349274324740)
XLA Ops:
  9.9 6.4 %copy.105 = bf16[1,4096,512]{1,2,0:T(8,128)(2,1)} copy(bf16[1,4096,512]{2,1,0:T(8,128)(2,1)} %param.23) | data formatting | bytes 8388608 | tf_op args[4]
  16.7 6.6 %copy.107 = bf16[1,4096,512]{1,2,0:T(8,128)(2,1)} copy(bf16[1,4096,512]{2,1,0:T(8,128)(2,1)} %param.24) | data formatting | bytes 8388608 | tf_op args[5]
  23.3 28.9 %while.14 = (s32[]{:T(128)}, f32[1,256,4,128]{1,3,2,0:T(8,128)S(1)}, f32[1,256,4]{1,2,0:T(4,128)S(1)}, f32[1,256,4]{1,2,0:T(4,128)S(1)}, s32[]{:T(128)}, /*index...) while((s32[]{:T(128)}, ...), condition=%wide.region_4.5_spmd, body=%wide.region_1.4_spmd.sunk | while | flops 275651584 | bytes 8731331 | solution.py:193
  26.3 1.8 fusion.87
  31.1 1.8 fusion.87
  35.9 1.9 fusion.87
  40.8 1.8 fusion.87
  45.6 1.8 fusion.87
  50.4 1.8 fusion.87
  56.1 14.5 %all-gather.6.cloned.1.call-done = bf16[2,1024,2048]{2,1,0:T(8,128)(2,1)} async-done(((bf16[2,256,2048]{2,1,0:T(8,128)(2,1)}), bf16[2,1024,2048]{2,1,0:T(8,128)(2,1)}) %all-gather.6.cloned.1.call-update) | async-done | bytes 8388624 | tf_op jit(solution)/shard_map/all_gather | solution.py:160
  70.6 3.0 constant_dynamic-slice_fusion
  75.5 24.9 %reduce-scatter.3.cloned.1.call-done = bf16[256,512]{1,0:T(8,128)(2,1)} async-done(((bf16[256,2048]{1,0:T(8,128)(2,1)}), bf16[256,512]{1,0:T(8,128)(2,1)}) %reduce-scatter.3.cloned.1.call-update) | async-done | bytes 262160 | tf_op jit(solution)/shard_map/reduce_scatter | solution.py:203
  101.5 5.8 %psum.28 = f32[256]{0:T(256)S(1)} all-reduce(f32[256]{0:T(256)S(1)} %multiply_reduce_fusion.3), channel_id=1, replica_groups=mesh['seq'=8,'tp'=4] {'tp'}, use_global_device_ids=true, to_apply=%region_10.11 | all-reduce | flops 256 | bytes 2048 | tf_op jit(solution)/shard_map/psum | solution.py:206
  109.2 51.9 %all-gather.12.cloned.1.call-done = bf16[2176,512]{1,0:T(8,128)(2,1)} async-done(((bf16[272,512]{1,0:T(8,128)(2,1)}), bf16[2176,512]{1,0:T(8,128)(2,1)}) %all-gather.12.cloned.1.call-update) | async-done | bytes 2228240 | tf_op jit(solution)/shard_map/all_gather | solution.py:64
  161.0 3.1 slice.40
  164.1 11.5 %copy.120 = bf16[2,2048,2,256]{1,3,2,0:T(8,128)(2,1)} copy(bf16[2,2048,2,256]{3,2,1,0:T(2,128)(2,1)} %param.30) | data formatting | bytes 8388608 | tf_op jit(solution)/shard_map/reshape | solution.py:71
  176.7 44.3 %all-gather.8.cloned.1.call-done = bf16[2048,2048]{1,0:T(8,128)(2,1)} async-done(((bf16[2048,512]{1,0:T(8,128)(2,1)}), bf16[2048,2048]{1,0:T(8,128)(2,1)}) %all-gather.8.cloned.1.call-update) | async-done | bytes 8388624 | tf_op jit(solution)/shard_map/all_gather | solution.py:70
  221.1 12.5 %fusion.31 = f32[2,2048,512]{1,2,0:T(8,128)S(1)} fusion(bf16[2,2048,512]{1,2,0:T(8,128)(2,1)} %bitcast.166, bf16[2048,2048]{1,0:T(8,128)(2,1)} %all-gather.8.cloned.1.call-done), kind=kOutput, calls=%fused_computation.39 | convolution fusion | flops 8589934592 | bytes 20971520 | tf_op jit(solution)/shard_map/td,edf->etf/dot_general | solution.py:72
  235.0 1.8 copy-done.2
  237.1 25.2 %collective-permute-done = bf16[2,2048,256]{1,2,0:T(8,128)(2,1)S(1)} collective-permute-done((bf16[2,2048,256]{1,2,0:T(8,128)(2,1)S(1)}, bf16[2,2048,256]{1,2,0:T(8,128)(2,1)S(1)}, u32[]{:S(2)}, u32[]{:S(2)}) %collective-permute-start) | collective-permute-done | bytes 2097184 | tf_op jit(solution)/shard_map/ppermute | solution.py:78
  262.3 25.6 %collective-permute-done.1 = bf16[2,2048,256]{1,2,0:T(8,128)(2,1)} collective-permute-done((bf16[2,2048,256]{1,2,0:T(8,128)(2,1)S(1)}, bf16[2,2048,256]{1,2,0:T(8,128)(2,1)}, u32[]{:S(2)}, u32[]{:S(2)}) %collective-permute-start.1) | collective-permute-done | bytes 2097184 | tf_op jit(solution)/shard_map/ppermute | solution.py:78
  287.9 25.8 %collective-permute-done.2 = bf16[2,2048,256]{1,2,0:T(8,128)(2,1)} collective-permute-done((bf16[2,2048,256]{1,2,0:T(8,128)(2,1)}, bf16[2,2048,256]{1,2,0:T(8,128)(2,1)}, u32[]{:S(2)}, u32[]{:S(2)}) %collective-permute-start.2) | collective-permute-done | bytes 2097184 | tf_op jit(solution)/shard_map/ppermute | solution.py:78
  313.6 1.9 constant_dynamic-update-slice_fusion.7
  315.5 2.0 constant_dynamic-update-slice_fusion.6
  324.8 5.8 %bitcast_convert_fusion = bf16[2048,512]{1,0:T(8,128)(2,1)} fusion(bf16[2,1024,512]{2,1,0:T(8,128)(2,1)S(1)} %copy-done.7, bf16[2,2048,2048]{1,2,0:T(8,128)(2,1)S(1)} %constant_dynamic-update-slice_fusion, s32[]{:T(128)S(6)} %select_n.59), kind=kOutput, calls=%fused_computation.42 | convolution fusion | flops 4296015872 | bytes 12582916 | tf_op jit(solution)/shard_map/etf,efd->td/dot_general | solution.py:82
  330.7 67.9 %reduce-scatter.5.cloned.1.call-done = bf16[256,512]{1,0:T(8,128)(2,1)} async-done(((bf16[2048,512]{1,0:T(8,128)(2,1)}), bf16[256,512]{1,0:T(8,128)(2,1)}) %reduce-scatter.5.cloned.1.call-update) | async-done | bytes 262160 | tf_op jit(solution)/shard_map/reduce_scatter | solution.py:85
  398.6 1.9 multiply_reduce_fusion.2
  400.5 8.9 %copy.115 = bf16[2048,3,512]{0,2,1:T(8,128)(2,1)} copy(bf16[2048,3,512]{2,0,1:T(8,128)(2,1)} %param.33) | data formatting | bytes 12582912 | tf_op args[14]
  409.4 7.0 %all-gather.10.cloned.1.call-done = bf16[256,2048]{1,0:T(8,128)(2,1)} async-done(((bf16[256,512]{1,0:T(8,128)(2,1)}), bf16[256,2048]{1,0:T(8,128)(2,1)}) %all-gather.10.cloned.1.call-update) | async-done | bytes 1048592 | tf_op jit(solution)/shard_map/all_gather | solution.py:224
  416.4 5.1 %fusion.29 = f32[256,3,512]{2,0,1:T(8,128)S(1)} fusion(bf16[2048,3,512]{0,2,1:T(8,128)(2,1)} %copy.115, bf16[256,2048]{1,0:T(8,128)(2,1)} %all-gather.10.cloned.1.call-done), kind=kOutput, calls=%fused_computation.37 | convolution fusion | flops 1610612736 | bytes 8912896 | tf_op jit(solution)/shard_map/dot_general | solution.py:223
  422.8 5.9 %all-reduce = (f32[256]{0:T(256)S(1)}, f32[256]{0:T(256)S(1)}, f32[256]{0:T(256)S(1)}) all-reduce(f32[256]{0:T(256)S(1)} %get-tuple-element.107, f32[256]{0:T(256)S(1)} %get-tuple-element.142, f32[256]{0:T(256)S(1)} %get-tuple-element.106), channel_id=1, replica_groups=mesh['seq'=8,'tp'=4] {'tp'}, use_global_device_ids=true, to_apply=%region_16.17 | all-reduce | flops 768 | bytes 6144 | tf_op jit(solution)/shard_map/psum | solution.py:230
  428.7 2.4 fusion.44
  (120 shorter events, 39.8 us)
Async XLA Ops:
  7.2 66.5 %copy-start = (bf16[512,2048]{1,0:T(8,128)(2,1)S(1)}, bf16[512,2048]{1,0:T(8,128)(2,1)}, u32[]{:S(2)}) copy-start(bf16[512,2048]{1,0:T(8,128)(2,1)} %param.26) | copy-start | bytes 6291460
  7.2 63.4 %all-gather.6.cloned.1.call-start = ((), (), s32[]{:S(2)}) async-start(), calls=%async_computation.2 | async-start | bytes 10485760 | tf_op jit(solution)/shard_map/all_gather | solution.py:160
  7.9 92.5 %reduce-scatter.3.cloned.1.call-start = ((), (), s32[]{:S(2)}) async-start(), calls=%async_computation.3 | async-start | bytes 1310720 | tf_op jit(solution)/shard_map/reduce_scatter | solution.py:203
  9.9 6.5 %copy-start.8 = (bf16[256,512]{1,0:T(8,128)(2,1)S(1)}, bf16[256,512]{1,0:T(8,128)(2,1)}, u32[]{:S(2)}) copy-start(bf16[256,512]{1,0:T(8,128)(2,1)} %param.20) | copy-start | bytes 786436
  56.1 19.3 %copy-start.9 = (f32[256,8]{0,1:T(8,128)S(1)}, f32[256,8]{0,1:T(8,128)}, u32[]{:S(2)}) copy-start(f32[256,8]{0,1:T(8,128)} %param.29) | copy-start | bytes 24580
  56.1 19.3 %copy-start.10 = (s32[256,8]{0,1:T(8,128)S(1)}, s32[256,8]{0,1:T(8,128)}, u32[]{:S(2)}) copy-start(s32[256,8]{0,1:T(8,128)} %param.28) | copy-start | bytes 24580
  56.1 44.3 %copy-start.5 = (bf16[256,512]{1,0:T(8,128)(2,1)S(1)}, bf16[256,512]{1,0:T(8,128)(2,1)}, u32[]{:S(2)}) copy-start(bf16[256,512]{1,0:T(8,128)(2,1)} %param.19) | copy-start | bytes 786436
  56.1 51.2 %copy-start.11 = (f32[512]{0:T(512)S(1)}, f32[512]{0:T(512)}, u32[]{:S(2)}) copy-start(f32[512]{0:T(512)} %param.27) | copy-start | bytes 6148
  75.3 85.7 %all-gather.12.cloned.1.call-start = ((), (), s32[]{:S(2)}) async-start(), calls=%async_computation.7 | async-start | bytes 2506752 | tf_op jit(solution)/shard_map/all_gather | solution.py:64
  109.1 111.9 %all-gather.8.cloned.1.call-start = ((), (), s32[]{:S(2)}) async-start(), calls=%async_computation.4 | async-start | bytes 10485760 | tf_op jit(solution)/shard_map/all_gather | solution.py:70
  164.1 234.5 %reduce-scatter.5.cloned.1.call-start = ((), (), s32[]{:S(2)}) async-start(), calls=%async_computation.5 | async-start | bytes 2359296 | tf_op jit(solution)/shard_map/reduce_scatter | solution.py:85
  233.6 3.2 copy-start.2
  236.8 25.5 %collective-permute-start = (bf16[2,2048,256]{1,2,0:T(8,128)(2,1)S(1)}, bf16[2,2048,256]{1,2,0:T(8,128)(2,1)S(1)}, u32[]{:S(2)}, u32[]{:S(2)}) collective-permute-start(bf16[2,2048,256]{1,2,0:T(8,128)(2,1)S(1)} %multiply_convert_fusion), channel_id=1, source_target_pairs={{0,1},{1,2},{2,3},{3,0},{4,5},{5,6},{6,7},{7,4},{8,9},{9,10},{10,1... | collective-permute-start | bytes 6291464 | tf_op jit(solution)/shard_map/ppermute | solution.py:78
  262.3 25.6 %collective-permute-start.1 = (bf16[2,2048,256]{1,2,0:T(8,128)(2,1)S(1)}, bf16[2,2048,256]{1,2,0:T(8,128)(2,1)}, u32[]{:S(2)}, u32[]{:S(2)}) collective-permute-start(bf16[2,2048,256]{1,2,0:T(8,128)(2,1)S(1)} %collective-permute-done), channel_id=1, source_target_pairs={{0,1},{1,2},{2,3},{3,0},{4,5},{5,6},{6,7},{7,4},{8,9},{9,10},{10,1... | collective-permute-start | bytes 6291464 | tf_op jit(solution)/shard_map/ppermute | solution.py:78
  287.8 25.8 %collective-permute-start.2 = (bf16[2,2048,256]{1,2,0:T(8,128)(2,1)}, bf16[2,2048,256]{1,2,0:T(8,128)(2,1)}, u32[]{:S(2)}, u32[]{:S(2)}) collective-permute-start(bf16[2,2048,256]{1,2,0:T(8,128)(2,1)} %collective-permute-done.1), channel_id=1, source_target_pairs={{0,1},{1,2},{2,3},{3,0},{4,5},{5,6},{6,7},{7,4},{8,9},{9,10},{10,1... | collective-permute-start | bytes 6291464 | tf_op jit(solution)/shard_map/ppermute | solution.py:78
  313.6 4.6 %copy-start.3 = (f32[2,2048,512]{1,2,0:T(8,128)S(1)}, f32[2,2048,512]{1,2,0:T(8,128)}, u32[]{:S(2)}) copy-start(f32[2,2048,512]{1,2,0:T(8,128)} %copy-done.2) | copy-start | bytes 25165828
  323.2 1.6 copy-start.7
  324.8 73.8 %copy-start.6 = (bf16[256,512]{1,0:T(8,128)(2,1)S(1)}, bf16[256,512]{1,0:T(8,128)(2,1)}, u32[]{:S(2)}) copy-start(bf16[256,512]{1,0:T(8,128)(2,1)} %reduce-scatter.3.cloned.1.call-done) | copy-start | bytes 786436
  324.8 73.8 %copy-start.12 = (f32[512]{0:T(512)S(1)}, f32[512]{0:T(512)}, u32[]{:S(2)}) copy-start(f32[512]{0:T(512)} %param.32) | copy-start | bytes 6148
  330.6 85.8 %all-gather.10.cloned.1.call-start = ((), (), s32[]{:S(2)}) async-start(), calls=%async_computation.6 | async-start | bytes 1310720 | tf_op jit(solution)/shard_map/all_gather | solution.py:224
  409.4 19.3 %copy-start.13 = (f32[512]{0:T(512)S(1)}, f32[512]{0:T(512)}, u32[]{:S(2)}) copy-start(f32[512]{0:T(512)} %param.35) | copy-start | bytes 6148
  409.4 19.3 %copy-start.14 = (f32[512]{0:T(512)S(1)}, f32[512]{0:T(512)}, u32[]{:S(2)}) copy-start(f32[512]{0:T(512)} %param.34) | copy-start | bytes 6148
  416.4 14.7 %copy-start.1 = (bf16[512,2048]{1,0:T(8,128)(2,1)S(1)}, bf16[512,2048]{1,0:T(8,128)(2,1)}, u32[]{:S(2)}) copy-start(bf16[512,2048]{1,0:T(8,128)(2,1)} %param.26) | copy-start | bytes 6291460
  421.5 1.2 copy-start.4
Sparse Core Ops, SparseCore 0:
  9.6 60.9 all-gather.5
  75.5 24.8 reduce-scatter.2
  109.2 51.7 all-gather.11
  164.2 56.7 all-gather.7
  330.7 67.8 reduce-scatter.4
  400.7 15.6 all-gather.9
